TPU v7x, 256 devices: a whole 4x4x8 slice. The times are simulated.
256 devices in a mesh: dp: 16 (over z, core), seq: 16 (over y, x).
Axes of the slice: x: 4, y: 4, z: 8, core: 2. Of those that a mesh axis runs over, the one named last changes fastest.
Arguments:
- clean_frames: bfloat16 [16, 2048, 1024], P('dp', 'seq')
- noise_frames: bfloat16 [16, 2048, 1024], P('dp', 'seq'), may hold values from -6 to 6
- lengths: int32 [16], P('dp'), may hold values from 512 to 2048
- group_ids: int32 [16, 2048], P('dp'), may hold values from 0 to 255, never falling along the last dimension, each value on 1 to 25 neighbouring positions
- time_index: int32 [16], P('dp'), may hold values from 0 to 999
- modulation: float32 [1024], replicated, may hold values from -4 to 4
- teacher_qkv: bfloat16 [1024, 3072], replicated, may hold values from -0.1875 to 0.1875
- teacher_out: bfloat16 [1024, 1024], replicated, may hold values from -6 to 6
- student_in: bfloat16 [3, 1024, 1024], P(None, ('dp', 'seq')), may hold values from -0.1875 to 0.1875
- student_out: bfloat16 [1024, 1024], P(('dp', 'seq')), may hold values from -1 to 1
Outputs:
- grad_inputs: float32 [2, 1024, 1024], P(None, ('dp', 'seq'))
- mean_error: float32 [], replicated
Inputs may be any that keep to these rules, and one draw needn't show every extreme that they name: `group_ids`: group numbers never fall along a dialogue, and each group holds 1 to 25 frames.
All inputs are finite; a program needn't handle non-finite values.
Results may differ from a plain program's by a relative error of at most 0.015.
Values may be sent and summed in bfloat16 or wider, within the bound.
No kernel may reach another device: no remote copies, remote signals or barrier semaphores. Data moves between devices by JAX's collectives and lax.ppermute only.
A program may use at most 128 MiB of HBM per device.

v0:
```python
import jax
import jax.numpy as jnp
from jax import lax
from jax.sharding import PartitionSpec as P

HEADS = 16
HALO = 64
TSTEPS = 1000
EPSILON = 1e-06
NEGATIVE = -1e30


def with_halo(block, sides, width):
    for axis, dim in sides:
        count = lax.axis_size(axis)
        forward = [(i, i + 1) for i in range(count - 1)]
        backward = [(target, source) for source, target in forward]
        low = lax.ppermute(
            lax.slice_in_dim(block, block.shape[dim] - width, None, axis=dim), axis, forward
        )
        high = lax.ppermute(lax.slice_in_dim(block, 0, width, axis=dim), axis, backward)
        block = jnp.concatenate([low, block, high], axis=dim)
    return block


def from_behind(block, axis, distance):
    devices = range(lax.axis_size(axis))
    route = [(i - distance, i) for i in devices if i - distance in devices]
    return lax.ppermute(block, axis, route)


def normalize(clean_frames, noise_frames, time_index, modulation):
    flow_time = (time_index.astype(jnp.float32) + 0.5) / TSTEPS
    flow_time = flow_time[:, None, None]
    blended = (1.0 - flow_time) * noise_frames.astype(
        jnp.float32
    ) + flow_time * clean_frames.astype(jnp.float32)
    inv_rms = lax.rsqrt(jnp.mean(blended * blended, axis=-1, keepdims=True) + EPSILON)
    return (blended * inv_rms * (1.0 + flow_time * modulation)).astype(jnp.bfloat16)


def attend_block(queries, key_rows, values, key_bias):
    scores = jnp.dot(queries, key_rows.T, preferred_element_type=jnp.float32) * queries.shape[
        -1
    ] ** (-0.5)
    scores = scores + key_bias[None, :]
    row_max = jnp.max(scores, axis=-1, keepdims=True)
    exponent = jnp.exp(scores - row_max)
    probs_low = (exponent / jnp.sum(exponent, axis=-1, keepdims=True)).astype(jnp.bfloat16)
    return jnp.dot(probs_low, values, preferred_element_type=jnp.float32).astype(jnp.bfloat16)


def full_attention(queries, key_rows, values, key_bias):
    total_rows = queries.shape[0]
    block_rows = min(512, total_rows)
    blocked = queries.reshape(total_rows // block_rows, block_rows, queries.shape[1])
    result = lax.map(lambda piece: attend_block(piece, key_rows, values, key_bias), blocked)
    return result.reshape(total_rows, values.shape[1])


def teacher_heads(proj_one, bias_one):
    stacked = jnp.transpose(proj_one, (2, 1, 0, 3))
    result = lax.map(
        lambda element: full_attention(element[0], element[1], element[2], bias_one), stacked
    )
    return jnp.transpose(result, (1, 0, 2))


def build_allowed(query_group, query_pos, key_group, key_pos, lengths):
    same_group = key_group[:, None, :] == query_group[:, :, None]
    prev_group = key_group[:, None, :] == query_group[:, :, None] - 1
    live_key = (key_pos[None, :] < lengths[:, None]) & (key_pos[None, :] >= 0)
    itself = key_pos[None, :] == query_pos[:, None]
    return (same_group | prev_group) & (live_key[:, None, :] | itself[None])


def split_product(form, gradient, other, first):
    upper_part = gradient.astype(jnp.bfloat16)
    lower_part = (gradient - upper_part.astype(jnp.float32)).astype(jnp.bfloat16)
    if first:
        return jnp.einsum(form, upper_part, other, preferred_element_type=jnp.float32) + jnp.einsum(
            form, lower_part, other, preferred_element_type=jnp.float32
        )
    return jnp.einsum(form, other, upper_part, preferred_element_type=jnp.float32) + jnp.einsum(
        form, other, lower_part, preferred_element_type=jnp.float32
    )


def total_of(value):
    spread = jnp.broadcast_to(value, (lax.axis_size("seq"), 128))
    spread = lax.all_to_all(spread, "seq", 0, 0, tiled=True).sum(0, keepdims=True)
    spread = jnp.broadcast_to(spread, (lax.axis_size("dp"), 128))
    spread = lax.all_to_all(spread, "dp", 0, 0, tiled=True).sum(0)
    return spread[0]


def shards(
    clean_frames,
    noise_frames,
    lengths,
    group_ids,
    time_index,
    modulation,
    teacher_qkv,
    teacher_out,
    student_in,
    student_out,
):
    dialogs, shard_rows, model_width = clean_frames.shape
    head_dim = model_width // HEADS
    seq_count = lax.axis_size("seq")
    seq_index = lax.axis_index("seq")
    frames = shard_rows * seq_count
    window = shard_rows + 2 * HALO
    rows_each = student_out.shape[0]
    stacked = jnp.concatenate((student_in.reshape(3 * rows_each, model_width), student_out), axis=0)
    gathered = lax.all_gather(lax.all_gather(stacked, "seq", axis=0), "dp", axis=0)
    gathered = gathered.reshape(-1, 4 * rows_each, model_width)
    w_inputs = (
        gathered[:, : 3 * rows_each]
        .reshape(-1, 3, rows_each, model_width)
        .transpose(1, 0, 2, 3)
        .reshape(3, -1, model_width)
    )
    w_output = gathered[:, 3 * rows_each :].reshape(-1, model_width)
    frame_count = jnp.sum(lax.all_gather(lengths, "dp", axis=0, tiled=True)).astype(jnp.float32)
    normed = normalize(clean_frames, noise_frames, time_index, modulation)
    flat_rows = normed.reshape(dialogs * shard_rows, model_width)
    frame_pos = jnp.arange(frames, dtype=jnp.int32)
    key_bias = jnp.where(frame_pos[None, :] < lengths[:, None], 0.0, NEGATIVE).astype(jnp.float32)
    teacher_proj = jnp.dot(flat_rows, teacher_qkv, preferred_element_type=jnp.float32).astype(
        jnp.bfloat16
    )
    teacher_proj = teacher_proj.reshape(dialogs, shard_rows, 3, HEADS, head_dim)
    by_heads = lax.all_to_all(teacher_proj, "seq", split_axis=3, concat_axis=1, tiled=True)
    head_out = lax.map(lambda element: teacher_heads(element[0], element[1]), (by_heads, key_bias))
    by_frames = lax.all_to_all(head_out, "seq", split_axis=1, concat_axis=2, tiled=True)
    teacher_vel = jnp.dot(
        by_frames.reshape(dialogs * shard_rows, model_width),
        teacher_out,
        preferred_element_type=jnp.float32,
    )
    offset = seq_index * shard_rows
    queries = jnp.dot(flat_rows, w_inputs[0], preferred_element_type=jnp.float32).astype(
        jnp.bfloat16
    )
    queries = queries.reshape(dialogs, shard_rows, HEADS, head_dim)
    key_local = jnp.dot(flat_rows, w_inputs[1], preferred_element_type=jnp.float32).astype(
        jnp.bfloat16
    )
    value_local = jnp.dot(flat_rows, w_inputs[2], preferred_element_type=jnp.float32).astype(
        jnp.bfloat16
    )
    both_local = jnp.concatenate((key_local, value_local), axis=-1).reshape(
        dialogs, shard_rows, 2 * model_width
    )
    both_window = with_halo(both_local, (("seq", 1),), HALO)
    key_rows = both_window[:, :, :model_width].reshape(dialogs, window, HEADS, head_dim)
    value_rows = both_window[:, :, model_width:].reshape(dialogs, window, HEADS, head_dim)
    group_pad = jnp.pad(group_ids, ((0, 0), (HALO, HALO)), constant_values=-10)
    key_group = lax.dynamic_slice_in_dim(group_pad, offset, window, 1)
    query_group = lax.dynamic_slice_in_dim(group_ids, offset, shard_rows, 1)
    query_pos = offset + jnp.arange(shard_rows, dtype=jnp.int32)
    key_pos = offset - HALO + jnp.arange(window, dtype=jnp.int32)
    allowed = build_allowed(query_group, query_pos, key_group, key_pos, lengths)
    scaling = head_dim ** (-0.5)
    scores = jnp.einsum("brhd,bwhd->bhrw", queries, key_rows, preferred_element_type=jnp.float32)
    scores = jnp.where(allowed[:, None], scores * scaling, NEGATIVE)
    row_max = jnp.max(scores, axis=-1, keepdims=True)
    exponent = jnp.exp(scores - row_max)
    probs = exponent / jnp.sum(exponent, axis=-1, keepdims=True)
    probs_low = probs.astype(jnp.bfloat16)
    student_mix = jnp.einsum(
        "bhrw,bwhd->brhd", probs_low, value_rows, preferred_element_type=jnp.float32
    ).astype(jnp.bfloat16)
    mix_flat = student_mix.reshape(dialogs * shard_rows, model_width)
    student_vel = jnp.dot(mix_flat, w_output, preferred_element_type=jnp.float32)
    query_valid = (query_pos[None, :] < lengths[:, None]).reshape(-1)
    difference = jnp.where(query_valid[:, None], student_vel - teacher_vel, 0.0)
    square_sum = total_of(jnp.sum(difference * difference))
    mean_error = square_sum / (frame_count * model_width)
    grad_vel = (difference * lax.rsqrt(frame_count)).astype(jnp.bfloat16)
    grad_mix = jnp.dot(grad_vel, w_output.T, preferred_element_type=jnp.float32).astype(
        jnp.bfloat16
    )
    grad_mix = grad_mix.reshape(dialogs, shard_rows, HEADS, head_dim)
    grad_prob = jnp.einsum(
        "brhd,bwhd->bhrw", grad_mix, value_rows, preferred_element_type=jnp.float32
    )
    grad_score = probs * (grad_prob - jnp.sum(probs * grad_prob, axis=-1, keepdims=True)) * scaling
    grad_key = split_product("bhrw,brhd->bwhd", grad_score, queries, True)
    grad_value = jnp.einsum(
        "bhrw,brhd->bwhd", probs_low, grad_mix, preferred_element_type=jnp.float32
    )
    grad_both = jnp.concatenate(
        (
            grad_key.reshape(dialogs, window, model_width),
            grad_value.reshape(dialogs, window, model_width),
        ),
        axis=-1,
    )
    from_next = from_behind(grad_both[:, :HALO].astype(jnp.bfloat16), "seq", -1).astype(jnp.float32)
    from_prev = from_behind(
        grad_both[:, HALO + shard_rows :].astype(jnp.bfloat16), "seq", 1
    ).astype(jnp.float32)
    owned_rows = grad_both[:, HALO : HALO + shard_rows]
    owned_rows = owned_rows.at[:, :HALO].add(from_prev)
    owned_rows = owned_rows.at[:, shard_rows - HALO :].add(from_next)
    by_head = owned_rows.reshape(shard_rows, 2, HEADS, head_dim).transpose(0, 2, 1, 3)
    head_grads = lax.all_to_all(by_head, "seq", split_axis=1, concat_axis=0, tiled=True)
    head_grads = head_grads.reshape(frames, 2 * head_dim)
    normed_all = lax.all_gather(flat_rows, "seq", axis=0, tiled=True)
    partial = split_product("rf,rg->fg", head_grads, normed_all, False)
    dp_count = lax.axis_size("dp")
    partial = partial.reshape(dp_count, seq_count, rows_each, 2 * head_dim)
    partial = lax.all_to_all(partial, "dp", split_axis=0, concat_axis=0, tiled=True).sum(0)
    mine = lax.all_to_all(partial, "seq", split_axis=0, concat_axis=0, tiled=True)
    mine = mine.reshape(HEADS, rows_each, 2, head_dim).transpose(2, 1, 0, 3)
    grad_inputs = mine.reshape(2, rows_each, model_width)
    return (grad_inputs, mean_error)


def solution(mesh):
    in_specs = (
        P("dp", "seq", None),
        P("dp", "seq", None),
        P("dp"),
        P("dp", None),
        P("dp"),
        P(),
        P(),
        P(),
        P(None, ("dp", "seq"), None),
        P(("dp", "seq"), None),
    )
    out_specs = (P(None, ("dp", "seq"), None), P())
    return jax.shard_map(shards, mesh=mesh, in_specs=in_specs, out_specs=out_specs, check_vma=False)
```

profile of v0, /device:TPU:1, one launch (start us, length us, event | category | flops | bytes accessed | tf_op | source)
XLA Modules:
  0.0 354.5 jit_solution(4930259637896913242)
XLA Ops:
  8.8 21.8 %all-gather.1 = bf16[256,1024]{1,0:T(8,128)(2,1)} all-gather(bf16[16,1024]{1,0:T(8,128)(2,1)S(1)} %pad_maximum_fusion.2), channel_id=3, replica_groups=mesh['dp'=16,'seq'=16] {'seq'}, dimensions={0}, use_global_device_ids=true | all-gather | bytes 557056 | tf_op jit(solution)/shard_map/all_gather | solution.py:117
  31.3 1.2 multiply_reduce_fusion.2
  33.2 1.2 multiply_convert_fusion.1
  34.4 3.9 %convolution_convert_fusion = bf16[128,3072]{1,0:T(8,128)(2,1)S(1)} fusion(bf16[1024,3072]{1,0:T(8,128)(2,1)} %param.22, bf16[1,128,1024]{2,1,0:T(8,128)(2,1)S(1)} %multiply_convert_fusion.1), kind=kOutput, calls=%fused_computation.23 | convolution fusion | flops 805699584 | bytes 7340032 | tf_op jit(solution)/shard_map/dot_general | solution.py:131
  38.3 1.2 copy.96
  39.5 2.1 copy.97
  41.6 4.7 %all-to-all-start = ((bf16[1,128,3,16,64]{1,4,2,0,3:T(8,128)(2,1)}), bf16[1,128,3,16,64]{1,4,2,0,3:T(8,128)(2,1)S(1)}, u32[]{:S(2)}, u32[]{:S(2)}) async-start(bf16[1,128,3,16,64]{1,4,2,0,3:T(8,128)(2,1)} %copy.97), calls=%async_computation | async-start | bytes 1572864 | tf_op jit(solution)/shard_map/all_to_all | solution.py:135
  47.9 8.9 %all-to-all-done = bf16[1,128,3,16,64]{1,4,2,0,3:T(8,128)(2,1)S(1)} async-done(((bf16[1,128,3,16,64]{1,4,2,0,3:T(8,128)(2,1)}), bf16[1,128,3,16,64]{1,4,2,0,3:T(8,128)(2,1)S(1)}, u32[]{:S(2)}, u32[]{:S(2)}) %all-to-all-start) | async-done | bytes 786464 | tf_op jit(solution)/shard_map/all_to_all | solution.py:135
  56.8 1.4 copy.98
  58.3 1.4 squeeze.46
  60.6 1.2 copy.113
  61.8 1.3 copy.100
  64.1 17.6 %while.29 = (s32[]{:T(128)}, bf16[4,512,64]{1,2,0:T(8,128)(2,1)}, bf16[4,512,64]{2,1,0:T(8,128)(2,1)S(1)}, bf16[2048,64]{1,0:T(8,128)(2,1)S(1)}, bf16[2048,64]{1,0:T(8,128)(2,1)}, /*index=5*/s32[]{:T(128)}, s32[]{:T(128)}) while((s32[]{:T(128)}, bf16[4,512,64]{1,2,0:T(8,128)(2,1)}, bf16[4,512,64]{2,1,0:T(8,128)(2,1)S(1)}, ...), condition=%wide.region_6.7_spmd.clone, body=%wide.region_3.6_spmd.clone.sunk | while | flops 281054208 | bytes 14658161 | solution.py:57
  66.6 1.9 fusion.101
  71.0 1.9 fusion.101
  75.4 1.9 fusion.101
  79.8 1.9 fusion.101
  81.7 2.0 copy.114
  83.7 3.3 reshape.458
  87.5 12.4 %reduce.14 = bf16[2048,64]{1,0:T(8,128)(2,1)} reduce(bf16[2048,1,1,64]{3,2,1,0:T(2,128)(2,1)S(1)} %bitcast.156, bf16[]{:T(256)} %broadcast.275), dimensions={1,2}, to_apply=%bitcast.107.reduce_sub_computation | reduce | bytes 524290
  99.9 2.2 reshape.459
  102.0 3.5 all-to-all-start.1
  106.9 21.3 %all-reduce.1 = s32[16]{0:T(128)S(1)} all-reduce(s32[16]{0:T(128)S(1)} %dynamic-update-slice.6), channel_id=1, replica_groups=mesh['dp'=16,'seq'=16] {'dp'}, use_global_device_ids=true, to_apply=%add.1 | all-reduce | flops 16 | bytes 128
  131.1 7.2 %copy.116 = bf16[256,12,1024]{2,0,1:T(8,128)(2,1)S(1)} copy(bf16[256,12,1024]{2,1,0:T(8,128)(2,1)} %bitcast.144) | data formatting | bytes 12582912
  138.3 3.4 fusion.64
  141.6 2.9 copy.93
  144.6 4.0 %squeeze.45 = bf16[1024,1024]{1,0:T(8,128)(2,1)} reshape(bf16[1,256,4,1024]{3,2,1,0:T(4,128)(2,1)} %copy.93) | data formatting | bytes 4194304 | tf_op jit(solution)/shard_map/squeeze | solution.py:151
  148.5 4.5 %copy.92 = bf16[1,256,4,1024]{3,2,1,0:T(4,128)(2,1)} copy(bf16[1,256,4,1024]{3,1,2,0:T(8,128)(2,1)} %get-tuple-element.142) | data formatting | bytes 4194304 | tf_op jit(solution)/shard_map/slice | solution.py:148
  153.1 4.0 %squeeze.44 = bf16[1024,1024]{1,0:T(8,128)(2,1)} reshape(bf16[1,256,4,1024]{3,2,1,0:T(4,128)(2,1)} %copy.92) | data formatting | bytes 4194304 | tf_op jit(solution)/shard_map/squeeze | solution.py:148
  157.1 2.2 convolution_convert_fusion.3
  160.7 4.0 %collective-permute-start = (bf16[1,64,2048]{2,1,0:T(8,128)(2,1)}, bf16[1,64,2048]{2,1,0:T(8,128)(2,1)}, u32[]{:S(2)}, u32[]{:S(2)}) collective-permute-start(bf16[1,64,2048]{2,1,0:T(8,128)(2,1)} %get-tuple-element.152), channel_id=1, source_target_pairs={{0,1},{1,2},{2,3},{3,4},{4,5},{5,6},{6,7},{7,8},{8,9},{9,10},{10,1... | collective-permute-start | bytes 786440 | tf_op jit(solution)/shard_map/ppermute | solution.py:18
  164.7 1.3 collective-permute-start.1
  166.0 3.0 copy.90
  168.9 4.2 %squeeze.43 = bf16[1024,1024]{1,0:T(8,128)(2,1)} reshape(bf16[1,256,4,1024]{3,2,1,0:T(4,128)(2,1)} %copy.90) | data formatting | bytes 4194304 | tf_op jit(solution)/shard_map/squeeze | solution.py:144
  173.1 2.0 convolution_convert_fusion.5
  176.0 4.6 %slice.137 = bf16[256,4,1024]{2,1,0:T(4,128)(2,1)} slice(bf16[256,16,1024]{2,1,0:T(8,128)(2,1)} %all-gather.8.cloned.1.call-done), slice={[0:256], [12:16], [0:1024]} | slice | bytes 4194304 | tf_op jit(solution)/shard_map/slice | solution.py:125
  180.6 4.0 %reshape.438 = bf16[1024,1024]{1,0:T(8,128)(2,1)} reshape(bf16[256,4,1024]{2,1,0:T(4,128)(2,1)} %slice.137) | data formatting | bytes 4194304 | tf_op jit(solution)/shard_map/reshape | solution.py:125
  187.0 3.2 fusion.68
  190.2 2.3 convolution_convert_fusion.2
  193.0 1.1 multiply_reduce_fusion.1
  195.1 1.8 fusion.70
  197.0 15.6 %fusion.38 = f32[16,64,256]{2,1,0:T(8,128)} fusion(bf16[128,16,64]{0,2,1:T(8,128)(2,1)S(1)} %bitcast.173, f32[16,128,256]{2,1,0:T(8,128)} %fusion.70, f32[16,128,256]{2,1,0:T(8,128)} %get-tuple-element.155, f32[16,128]{1,0:T(8,128)S(1)} %get-tuple-element.154), kind=kOutput, calls=%fused_computation.61 | convolution fusion | flops 70781184 | bytes 5513216 | tf_op jit(solution)/shard_map/bhrw,brhd->bwhd/dot_general | solution.py:81
  212.6 14.9 %convolution_add_fusion = f32[16,64,256]{2,1,0:T(8,128)S(1)} fusion(f32[16,64,256]{2,1,0:T(8,128)} %fusion.38, bf16[128,16,64]{0,2,1:T(8,128)(2,1)} %bitcast.172, f32[16,128,256]{2,1,0:T(8,128)} %fusion.70, f32[16,128,256]{2,1,0:T(8,128)} %get-tuple-element.155, f32[16,128]{1,0:T(8,128)S(1)} %get-tuple-element.154), kind=kOutput, calls=%fused_computation.37 | convolution fusion | flops 72616192 | bytes 6561792 | tf_op jit(solution)/shard_map/bhrw,brhd->bwhd/dot_general | solution.py:81
  227.6 2.1 fusion.48
  230.9 4.0 %collective-permute-start.2 = (bf16[1,64,2048]{1,2,0:T(8,128)(2,1)S(1)}, bf16[1,64,2048]{1,2,0:T(8,128)(2,1)S(1)}, u32[]{:S(2)}, u32[]{:S(2)}) collective-permute-start(bf16[1,64,2048]{1,2,0:T(8,128)(2,1)S(1)} %get-tuple-element.146), channel_id=1, source_target_pairs={{0,1},{1,2},{2,3},{3,4},{4,5},{5,6},{6,7},{7,8},{8,9},{9,10},{10,1... | collective-permute-start | bytes 786440 | tf_op jit(solution)/shard_map/ppermute | solution.py:29
  234.9 1.3 collective-permute-start.3
  236.2 1.3 fusion.29
  237.5 5.9 %collective-permute-done.2 = bf16[1,64,2048]{1,2,0:T(8,128)(2,1)S(1)} collective-permute-done((bf16[1,64,2048]{1,2,0:T(8,128)(2,1)S(1)}, bf16[1,64,2048]{1,2,0:T(8,128)(2,1)S(1)}, u32[]{:S(2)}, u32[]{:S(2)}) %collective-permute-start.2) | collective-permute-done | bytes 262176 | tf_op jit(solution)/shard_map/ppermute | solution.py:29
  243.4 1.4 fusion.31
  244.7 5.7 %scatter-add.6 = f32[1,128,2048]{1,2,0:T(8,128)} dynamic-update-slice(f32[1,128,2048]{1,2,0:T(8,128)} %fusion.29, f32[1,64,2048]{1,2,0:T(8,128)} %fusion.31, s32[]{:T(128)} %constant.131.clone.1, s32[]{:T(128)} %constant.131.clone.1, s32[]{:T(128)} %constant.131.clone.1) | dynamic-update-slice | bytes 1048580 | tf_op jit(solution)/shard_map/scatter-add | solution.py:207
  250.4 2.8 slice_add_fusion
  253.2 8.6 %scatter-add.9 = f32[1,128,2048]{1,2,0:T(8,128)S(1)} dynamic-update-slice(f32[1,128,2048]{1,2,0:T(8,128)S(1)} %copy-done.5, f32[1,64,2048]{1,2,0:T(8,128)} %slice_add_fusion, s32[]{:T(128)} %constant.131.clone.1, s32[]{:T(128)} %constant.142.clone.1, s32[]{:T(128)} %constant.131.clone.1) | dynamic-update-slice | bytes 1048580 | tf_op jit(solution)/shard_map/scatter-add | solution.py:208
  262.0 21.2 %all_to_all.67 = f32[128,16,2,64]{0,3,2,1:T(8,128)} all-to-all(f32[128,16,2,64]{0,3,2,1:T(8,128)S(1)} %copy.107), channel_id=1, replica_groups=mesh['dp'=16,'seq'=16] {'seq'}, dimensions={1} | all-to-all | bytes 2097152 | tf_op jit(solution)/shard_map/all_to_all | solution.py:210
  283.2 1.2 broadcast_in_dim.59
  284.5 3.5 all-to-all-start.5
  287.9 1.8 copy.108
  289.8 3.7 %fusion.16 = f32[1024,128]{1,0:T(8,128)S(1)} fusion(bf16[1,2048,1024]{2,1,0:T(8,128)(2,1)} %all-gather.6.cloned.1.call-done, f32[16,8,16,128]{3,2,1,0:T(8,128)S(1)} %bitcast.152), kind=kOutput, calls=%fused_computation.19 | convolution fusion | flops 537919488 | bytes 5767168 | tf_op jit(solution)/shard_map/rf,rg->fg/dot_general | solution.py:84
  293.5 2.3 fusion.25
  295.8 8.3 %all-to-all-start.3 = ((f32[16,16,4,128]{3,2,1,0:T(4,128)}), f32[16,16,4,128]{3,2,1,0:T(4,128)S(1)}, u32[]{:S(2)}, u32[]{:S(2)}) async-start(f32[16,16,4,128]{3,2,1,0:T(4,128)} %bitcast.164), calls=%async_computation.3 | async-start | bytes 1048576 | tf_op jit(solution)/shard_map/all_to_all | solution.py:216
  304.2 17.3 %all-to-all-done.3 = f32[16,16,4,128]{3,2,1,0:T(4,128)S(1)} async-done(((f32[16,16,4,128]{3,2,1,0:T(4,128)}), f32[16,16,4,128]{3,2,1,0:T(4,128)S(1)}, u32[]{:S(2)}, u32[]{:S(2)}) %all-to-all-start.3) | async-done | bytes 524320 | tf_op jit(solution)/shard_map/all_to_all | solution.py:216
  322.1 3.3 all-to-all-start.6
  326.1 5.9 %all-to-all-done.6 = f32[16,1,128]{2,1,0:T(1,128)S(1)} async-done(((f32[16,1,128]{2,1,0:T(1,128)}), f32[16,1,128]{2,1,0:T(1,128)S(1)}, u32[]{:S(2)}, u32[]{:S(2)}) %all-to-all-start.6) | async-done | bytes 8224 | tf_op jit(solution)/shard_map/all_to_all | solution.py:93
  332.1 6.9 %all-to-all-start.4 = ((f32[16,4,128]{2,1,0:T(4,128)}), f32[16,4,128]{2,1,0:T(4,128)S(1)}, u32[]{:S(2)}, u32[]{:S(2)}) async-start(f32[16,4,128]{2,1,0:T(4,128)} %reduce_sum.85), calls=%async_computation.4 | async-start | bytes 65536 | tf_op jit(solution)/shard_map/all_to_all | solution.py:217
  339.0 6.4 %all-to-all-done.4 = f32[16,4,128]{2,1,0:T(4,128)S(1)} async-done(((f32[16,4,128]{2,1,0:T(4,128)}), f32[16,4,128]{2,1,0:T(4,128)S(1)}, u32[]{:S(2)}, u32[]{:S(2)}) %all-to-all-start.4) | async-done | bytes 32800 | tf_op jit(solution)/shard_map/all_to_all | solution.py:217
  (97 shorter events, 28.6 us)
Async XLA Ops:
  7.2 185.8 %copy-start = (bf16[1024,1024]{1,0:T(8,128)(2,1)S(1)}, bf16[1024,1024]{1,0:T(8,128)(2,1)}, u32[]{:S(2)}) copy-start(bf16[1024,1024]{1,0:T(8,128)(2,1)} %param.23) | copy-start | bytes 6291460
  7.2 123.9 %all-gather.8.cloned.1.call-start = ((), (), s32[]{:S(2)}) async-start(), calls=%async_computation.8 | async-start | bytes 8912896 | tf_op jit(solution)/shard_map/all_gather | solution.py:117
  34.4 3.9 %copy-start.3 = (bf16[1,128,1024]{2,1,0:T(8,128)(2,1)}, bf16[1,128,1024]{2,1,0:T(8,128)(2,1)S(1)}, u32[]{:S(2)}) copy-start(bf16[1,128,1024]{2,1,0:T(8,128)(2,1)S(1)} %multiply_convert_fusion.1) | copy-start | bytes 786436
  39.5 8.3 %copy-start.10 = (s32[1,2048]{1,0:T(1,128)S(1)}, s32[1,2048]{1,0:T(1,128)}, u32[]{:S(2)}) copy-start(s32[1,2048]{1,0:T(1,128)} %param.19) | copy-start | bytes 24580
  41.6 15.2 %all-to-all-start = ((bf16[1,128,3,16,64]{1,4,2,0,3:T(8,128)(2,1)}), bf16[1,128,3,16,64]{1,4,2,0,3:T(8,128)(2,1)S(1)}, u32[]{:S(2)}, u32[]{:S(2)}) async-start(bf16[1,128,3,16,64]{1,4,2,0,3:T(8,128)(2,1)} %copy.97), calls=%async_computation | async-start | bytes 1572864 | tf_op jit(solution)/shard_map/all_to_all | solution.py:135
  46.4 243.4 %all-gather.6.cloned.1.call-start = ((), (), s32[]{:S(2)}) async-start(), calls=%async_computation.7 | async-start | bytes 4456448 | tf_op jit(solution)/shard_map/all_gather | solution.py:212
  65.6 1.0 copy-start.8
  70.0 1.0 copy-start.8
  74.3 1.1 copy-start.8
  78.7 1.1 copy-start.8
  83.7 21.9 %copy-start.11 = (u32[256]{0:T(256)S(1)}, u32[256]{0:T(256)}, u32[]{:S(2)}) copy-start(u32[256]{0:T(256)} %constant.155) | copy-start | bytes 3076
  102.0 27.6 %all-to-all-start.1 = ((bf16[16,2,4096]{2,1,0:T(2,128)(2,1)}), bf16[16,2,4096]{2,1,0:T(2,128)(2,1)S(1)}, u32[]{:S(2)}, u32[]{:S(2)}) async-start(bf16[16,2,4096]{2,1,0:T(2,128)(2,1)} %reshape.459), calls=%async_computation.1 | async-start | bytes 524288 | tf_op jit(solution)/shard_map/all_to_all | solution.py:137
  153.1 4.0 %copy-start.4 = (bf16[1,128,1024]{2,1,0:T(8,128)(2,1)S(1)}, bf16[1,128,1024]{2,1,0:T(8,128)(2,1)}, u32[]{:S(2)}) copy-start(bf16[1,128,1024]{2,1,0:T(8,128)(2,1)} %copy-done.3) | copy-start | bytes 786436
  157.1 2.2 copy-start.6
  159.3 6.6 %copy-start.7 = (bf16[1,256,4,1024]{3,1,2,0:T(8,128)(2,1)S(1)}, bf16[1,256,4,1024]{3,1,2,0:T(8,128)(2,1)}, u32[]{:S(2)}) copy-start(bf16[1,256,4,1024]{3,1,2,0:T(8,128)(2,1)} %get-tuple-element.144) | copy-start | bytes 6291460
  160.7 23.9 %collective-permute-start = (bf16[1,64,2048]{2,1,0:T(8,128)(2,1)}, bf16[1,64,2048]{2,1,0:T(8,128)(2,1)}, u32[]{:S(2)}, u32[]{:S(2)}) collective-permute-start(bf16[1,64,2048]{2,1,0:T(8,128)(2,1)} %get-tuple-element.152), channel_id=1, source_target_pairs={{0,1},{1,2},{2,3},{3,4},{4,5},{5,6},{6,7},{7,8},{8,9},{9,10},{10,1... | collective-permute-start | bytes 786440 | tf_op jit(solution)/shard_map/ppermute | solution.py:18
  164.7 19.9 %collective-permute-start.1 = (bf16[1,64,2048]{2,1,0:T(8,128)(2,1)}, bf16[1,64,2048]{2,1,0:T(8,128)(2,1)}, u32[]{:S(2)}, u32[]{:S(2)}) collective-permute-start(bf16[1,64,2048]{2,1,0:T(8,128)(2,1)} %get-tuple-element.153), channel_id=1, source_target_pairs={{1,0},{2,1},{3,2},{4,3},{5,4},{6,5},{7,6},{8,7},{9,8},{10,9},{11,1... | collective-permute-start | bytes 786440 | tf_op jit(solution)/shard_map/ppermute | solution.py:21
  190.2 2.3 copy-start.2
  194.9 2.0 copy-start.9
  230.9 12.5 %collective-permute-start.2 = (bf16[1,64,2048]{1,2,0:T(8,128)(2,1)S(1)}, bf16[1,64,2048]{1,2,0:T(8,128)(2,1)S(1)}, u32[]{:S(2)}, u32[]{:S(2)}) collective-permute-start(bf16[1,64,2048]{1,2,0:T(8,128)(2,1)S(1)} %get-tuple-element.146), channel_id=1, source_target_pairs={{0,1},{1,2},{2,3},{3,4},{4,5},{5,6},{6,7},{7,8},{8,9},{9,10},{10,1... | collective-permute-start | bytes 786440 | tf_op jit(solution)/shard_map/ppermute | solution.py:29
  234.9 15.6 %collective-permute-start.3 = (bf16[1,64,2048]{1,2,0:T(8,128)(2,1)}, bf16[1,64,2048]{1,2,0:T(8,128)(2,1)}, u32[]{:S(2)}, u32[]{:S(2)}) collective-permute-start(bf16[1,64,2048]{1,2,0:T(8,128)(2,1)} %get-tuple-element.145), channel_id=1, source_target_pairs={{1,0},{2,1},{3,2},{4,3},{5,4},{6,5},{7,6},{8,7},{9,8},{10,9},{11,1... | collective-permute-start | bytes 786440 | tf_op jit(solution)/shard_map/ppermute | solution.py:29
  250.4 2.8 copy-start.5
  284.5 11.3 %all-to-all-start.5 = ((f32[16,1,128]{2,1,0:T(1,128)}), f32[16,1,128]{2,1,0:T(1,128)S(1)}, u32[]{:S(2)}, u32[]{:S(2)}) async-start(f32[16,1,128]{2,1,0:T(1,128)} %broadcast_in_dim.59), calls=%async_computation.5 | async-start | bytes 16384 | tf_op jit(solution)/shard_map/all_to_all | solution.py:91
  289.8 3.7 %copy-start.1 = (bf16[1,2048,1024]{2,1,0:T(8,128)(2,1)S(1)}, bf16[1,2048,1024]{2,1,0:T(8,128)(2,1)}, u32[]{:S(2)}) copy-start(bf16[1,2048,1024]{2,1,0:T(8,128)(2,1)} %all-gather.6.cloned.1.call-done) | copy-start | bytes 12582916
  295.8 25.7 %all-to-all-start.3 = ((f32[16,16,4,128]{3,2,1,0:T(4,128)}), f32[16,16,4,128]{3,2,1,0:T(4,128)S(1)}, u32[]{:S(2)}, u32[]{:S(2)}) async-start(f32[16,16,4,128]{3,2,1,0:T(4,128)} %bitcast.164), calls=%async_computation.3 | async-start | bytes 1048576 | tf_op jit(solution)/shard_map/all_to_all | solution.py:216
  322.1 10.0 %all-to-all-start.6 = ((f32[16,1,128]{2,1,0:T(1,128)}), f32[16,1,128]{2,1,0:T(1,128)S(1)}, u32[]{:S(2)}, u32[]{:S(2)}) async-start(f32[16,1,128]{2,1,0:T(1,128)} %broadcast_in_dim.88), calls=%async_computation.6 | async-start | bytes 16384 | tf_op jit(solution)/shard_map/all_to_all | solution.py:93
  332.1 13.3 %all-to-all-start.4 = ((f32[16,4,128]{2,1,0:T(4,128)}), f32[16,4,128]{2,1,0:T(4,128)S(1)}, u32[]{:S(2)}, u32[]{:S(2)}) async-start(f32[16,4,128]{2,1,0:T(4,128)} %reduce_sum.85), calls=%async_computation.4 | async-start | bytes 65536 | tf_op jit(solution)/shard_map/all_to_all | solution.py:217
Sparse Core Ops, SparseCore 0:
  30.7 62.3 all-gather.7
  95.6 56.0 all-gather.5
where the time goes:
time: 359 us; the launch traced here: 354 us
  local copies, waits for them, and re-layouts  87.6 us (24%)
  matrix products  67.7 us (19%)
  blocking collectives  64.3 us (18%)
  waiting for transfers between devices  44.6 us (12%)
  starting transfers between devices  41.5 us (12%)
  other arithmetic  30.8 us (9%)
  between operations  18 us (5%)
    all_gather x1, blocking collectives, shards(): lax.all_gather(stacked, 'seq', axis=0)  21.8 us
    unnamed x1, blocking collectives  21.3 us
    all_to_all x1, blocking collectives, shards(): lax.all_to_all(by_head, 'seq', split_axis=1, concat_axis=0, tiled=True)  21.2 us
    all_to_all x1, waiting for transfers between devices, shards(): lax.all_to_all(partial, 'dp', split_axis=0, concat_axis=0, tiled=True)  17.3 us
    dot_general x1, matrix products, split_product(): jnp.einsum(form, upper_part, other, preferred_element_type=jnp.float32)  15.6 us
    unnamed x33, local copies, waits for them, and re-layouts  15.5 us
    dot_general x1, matrix products, split_product(): jnp.einsum(form, lower_part, other, preferred_element_type=jnp.float32)  14.9 us
    unnamed x1, other arithmetic  12.4 us
  transfers between devices with their start and end apart: 12, of which 5 were waited for; matrix products, arithmetic and copies ran while one was open for 51% of the time, Pallas kernels for 0%

commit v1 on v0

--- a/solution.py
+++ b/solution.py
@@ -132,7 +132,12 @@
         jnp.bfloat16
     )
     teacher_proj = teacher_proj.reshape(dialogs, shard_rows, 3, HEADS, head_dim)
-    by_heads = lax.all_to_all(teacher_proj, "seq", split_axis=3, concat_axis=1, tiled=True)
+    by_heads = jnp.concatenate(
+        lax.all_to_all(
+            jnp.stack(jnp.split(teacher_proj, lax.axis_size("seq"), axis=3)), "seq", 0, 0
+        ),
+        axis=1,
+    )
     head_out = lax.map(lambda element: teacher_heads(element[0], element[1]), (by_heads, key_bias))
     by_frames = lax.all_to_all(head_out, "seq", split_axis=1, concat_axis=2, tiled=True)
     teacher_vel = jnp.dot(

time: 359 us -> 381 us (1.061)
  local copies, waits for them, and re-layouts: 87.6 us -> 107 us
    unnamed x33 -> x48, local copies, waits for them, and re-layouts: 15.5 us -> 35.4 us
  transfers between devices with their start and end apart: 12 -> 12, of which waited for: 5 -> 5; matrix products, arithmetic and copies ran while one was open for 51% -> 54% of each run, Pallas kernels for 0% -> 0%
where the time goes in v1:
time: 381 us; the launch traced here: 375 us
  local copies, waits for them, and re-layouts  107 us (28%)
  matrix products  67.7 us (18%)
  blocking collectives  65.1 us (17%)
  waiting for transfers between devices  44.3 us (12%)
  starting transfers between devices  41.9 us (11%)
  other arithmetic  30.8 us (8%)
  between operations  18 us (5%)
    unnamed x48, local copies, waits for them, and re-layouts  35.4 us
    all_to_all x1, blocking collectives, shards(): lax.all_to_all(by_head, 'seq', split_axis=1, concat_axis=0, tiled=True)  22 us
    all_gather x1, blocking collectives, shards(): lax.all_gather(stacked, 'seq', axis=0)  21.8 us
    unnamed x1, blocking collectives  21.4 us
    all_to_all x1, waiting for transfers between devices, shards(): lax.all_to_all(partial, 'dp', split_axis=0, concat_axis=0, tiled=True)  17.3 us
    dot_general x1, matrix products, split_product(): jnp.einsum(form, upper_part, other, preferred_element_type=jnp.float32)  15.6 us
    dot_general x1, matrix products, split_product(): jnp.einsum(form, lower_part, other, preferred_element_type=jnp.float32)  14.9 us
    unnamed x1, other arithmetic  12.4 us
  transfers between devices with their start and end apart: 12, of which 5 were waited for; matrix products, arithmetic and copies ran while one was open for 54% of the time, Pallas kernels for 0%

profile of v1, /device:TPU:1, one launch (start us, length us, event | category | flops | bytes accessed | tf_op | source)
XLA Modules:
  0.0 375.2 jit_solution(11478219585746661527)
XLA Ops:
  8.8 21.8 %all-gather.1 = bf16[256,1024]{1,0:T(8,128)(2,1)} all-gather(bf16[16,1024]{1,0:T(8,128)(2,1)S(1)} %pad_maximum_fusion.2), channel_id=3, replica_groups=mesh['dp'=16,'seq'=16] {'seq'}, dimensions={0}, use_global_device_ids=true | all-gather | bytes 557056 | tf_op jit(solution)/shard_map/all_gather | solution.py:117
  34.4 3.9 %convolution_convert_fusion = bf16[128,3072]{1,0:T(8,128)(2,1)S(1)} fusion(bf16[1024,3072]{1,0:T(8,128)(2,1)} %param.22, bf16[1,128,1024]{2,1,0:T(8,128)(2,1)S(1)} %multiply_convert_fusion.1), kind=kOutput, calls=%fused_computation.23 | convolution fusion | flops 805699584 | bytes 7340032 | tf_op jit(solution)/shard_map/dot_general | solution.py:131
  39.5 1.4 fusion.73
  40.9 1.4 fusion.72
  42.3 1.4 fusion.71
  45.2 1.4 fusion.69
  46.6 1.4 fusion.68
  48.0 1.4 fusion.67
  49.4 1.4 fusion.66
  50.9 1.4 fusion.65
  52.3 1.4 fusion.64
  62.2 4.8 %all-to-all-start = ((bf16[16,1,128,3,1,64]{2,5,3,4,1,0:T(8,128)(2,1)}), bf16[16,1,128,3,1,64]{2,5,3,4,1,0:T(8,128)(2,1)S(1)}, u32[]{:S(2)}, u32[]{:S(2)}) async-start(bf16[16,1,128,3,1,64]{2,5,3,4,1,0:T(8,128)(2,1)} %fusion.58), calls=%async_computation | async-start | bytes 1572864 | tf_op jit(solution)/shard_map/all_to_all | solution.py:136
  68.5 8.9 %all-to-all-done = bf16[16,1,128,3,1,64]{2,5,3,4,1,0:T(8,128)(2,1)S(1)} async-done(((bf16[16,1,128,3,1,64]{2,5,3,4,1,0:T(8,128)(2,1)}), bf16[16,1,128,3,1,64]{2,5,3,4,1,0:T(8,128)(2,1)S(1)}, u32[]{:S(2)}, u32[]{:S(2)}) %all-to-all-start) | async-done | bytes 786464 | tf_op jit(solution)/shard_map/all_to_all | solution.py:136
  77.4 1.4 copy.185
  78.9 1.4 squeeze.46
  81.1 2.0 copy.188
  83.6 17.6 %while.29 = (s32[]{:T(128)}, bf16[4,512,64]{1,2,0:T(8,128)(2,1)}, bf16[4,512,64]{2,1,0:T(8,128)(2,1)S(1)}, bf16[2048,64]{1,0:T(8,128)(2,1)S(1)}, bf16[2048,64]{1,0:T(8,128)(2,1)}, /*index=5*/s32[]{:T(128)}, s32[]{:T(128)}) while((s32[]{:T(128)}, bf16[4,512,64]{1,2,0:T(8,128)(2,1)}, bf16[4,512,64]{2,1,0:T(8,128)(2,1)S(1)}, ...), condition=%wide.region_6.7_spmd.clone, body=%wide.region_3.6_spmd.clone.sunk | while | flops 281054208 | bytes 14657661 | solution.py:57
  86.1 1.9 fusion.117
  90.5 1.9 fusion.117
  94.9 1.9 fusion.117
  99.3 1.9 fusion.117
  101.2 2.0 copy.201
  103.2 3.3 reshape.459
  107.0 12.4 %reduce.14 = bf16[2048,64]{1,0:T(8,128)(2,1)} reduce(bf16[2048,1,1,64]{3,2,1,0:T(2,128)(2,1)S(1)} %bitcast.247, bf16[]{:T(256)} %broadcast.275), dimensions={1,2}, to_apply=%bitcast.198.reduce_sub_computation | reduce | bytes 524290
  119.3 2.2 reshape.460
  121.5 3.5 all-to-all-start.1
  126.4 21.4 %all-reduce.1 = s32[16]{0:T(128)S(1)} all-reduce(s32[16]{0:T(128)S(1)} %dynamic-update-slice.6), channel_id=1, replica_groups=mesh['dp'=16,'seq'=16] {'dp'}, use_global_device_ids=true, to_apply=%add.1 | all-reduce | flops 16 | bytes 128
  150.7 6.9 %copy.203 = bf16[256,12,1024]{2,0,1:T(8,128)(2,1)S(1)} copy(bf16[256,12,1024]{2,1,0:T(8,128)(2,1)} %bitcast.235) | data formatting | bytes 12582912
  157.6 3.0 fusion.80
  160.5 4.6 %slice.137 = bf16[256,4,1024]{2,1,0:T(4,128)(2,1)} slice(bf16[256,16,1024]{2,1,0:T(8,128)(2,1)} %all-gather.8.cloned.1.call-done), slice={[0:256], [12:16], [0:1024]} | slice | bytes 4194304 | tf_op jit(solution)/shard_map/slice | solution.py:125
  165.1 4.0 %reshape.439 = bf16[1024,1024]{1,0:T(8,128)(2,1)} reshape(bf16[256,4,1024]{2,1,0:T(4,128)(2,1)} %slice.137) | data formatting | bytes 4194304 | tf_op jit(solution)/shard_map/reshape | solution.py:125
  169.1 4.5 %copy.165 = bf16[1,256,4,1024]{3,2,1,0:T(4,128)(2,1)} copy(bf16[1,256,4,1024]{3,1,2,0:T(8,128)(2,1)} %get-tuple-element.142) | data formatting | bytes 4194304 | tf_op jit(solution)/shard_map/slice | solution.py:153
  173.6 3.9 %squeeze.44 = bf16[1024,1024]{1,0:T(8,128)(2,1)} reshape(bf16[1,256,4,1024]{3,2,1,0:T(4,128)(2,1)} %copy.165) | data formatting | bytes 4194304 | tf_op jit(solution)/shard_map/squeeze | solution.py:153
  177.6 4.5 %copy.166 = bf16[1,256,4,1024]{3,2,1,0:T(4,128)(2,1)} copy(bf16[1,256,4,1024]{3,1,2,0:T(8,128)(2,1)} %get-tuple-element.143) | data formatting | bytes 4194304 | tf_op jit(solution)/shard_map/slice | solution.py:156
  182.1 4.0 %squeeze.45 = bf16[1024,1024]{1,0:T(8,128)(2,1)} reshape(bf16[1,256,4,1024]{3,2,1,0:T(4,128)(2,1)} %copy.166) | data formatting | bytes 4194304 | tf_op jit(solution)/shard_map/squeeze | solution.py:156
  186.1 2.2 convolution_convert_fusion.4
  189.7 4.1 %collective-permute-start = (bf16[1,64,2048]{2,1,0:T(8,128)(2,1)}, bf16[1,64,2048]{2,1,0:T(8,128)(2,1)}, u32[]{:S(2)}, u32[]{:S(2)}) collective-permute-start(bf16[1,64,2048]{2,1,0:T(8,128)(2,1)} %get-tuple-element.152), channel_id=1, source_target_pairs={{0,1},{1,2},{2,3},{3,4},{4,5},{5,6},{6,7},{7,8},{8,9},{9,10},{10,1... | collective-permute-start | bytes 786440 | tf_op jit(solution)/shard_map/ppermute | solution.py:18
  193.8 1.5 collective-permute-start.1
  195.3 2.9 copy.163
  198.3 4.0 %squeeze.43 = bf16[1024,1024]{1,0:T(8,128)(2,1)} reshape(bf16[1,256,4,1024]{3,2,1,0:T(4,128)(2,1)} %copy.163) | data formatting | bytes 4194304 | tf_op jit(solution)/shard_map/squeeze | solution.py:149
  202.2 2.0 convolution_convert_fusion.5
  207.5 3.2 fusion.84
  210.7 2.3 convolution_convert_fusion.2
  215.6 1.8 fusion.86
  217.5 15.6 %fusion.38 = f32[16,64,256]{2,1,0:T(8,128)} fusion(bf16[128,16,64]{0,2,1:T(8,128)(2,1)S(1)} %bitcast.278, f32[16,128,256]{2,1,0:T(8,128)} %fusion.86, f32[16,128,256]{2,1,0:T(8,128)} %get-tuple-element.155, f32[16,128]{1,0:T(8,128)S(1)} %get-tuple-element.154), kind=kOutput, calls=%fused_computation.61 | convolution fusion | flops 70781184 | bytes 5513216 | tf_op jit(solution)/shard_map/bhrw,brhd->bwhd/dot_general | solution.py:81
  233.1 14.9 %convolution_add_fusion = f32[16,64,256]{2,1,0:T(8,128)S(1)} fusion(f32[16,64,256]{2,1,0:T(8,128)} %fusion.38, bf16[128,16,64]{0,2,1:T(8,128)(2,1)} %bitcast.277, f32[16,128,256]{2,1,0:T(8,128)} %fusion.86, f32[16,128,256]{2,1,0:T(8,128)} %get-tuple-element.155, f32[16,128]{1,0:T(8,128)S(1)} %get-tuple-element.154), kind=kOutput, calls=%fused_computation.37 | convolution fusion | flops 72616192 | bytes 6561792 | tf_op jit(solution)/shard_map/bhrw,brhd->bwhd/dot_general | solution.py:81
  248.1 2.1 fusion.48
  251.4 4.0 %collective-permute-start.2 = (bf16[1,64,2048]{1,2,0:T(8,128)(2,1)S(1)}, bf16[1,64,2048]{1,2,0:T(8,128)(2,1)S(1)}, u32[]{:S(2)}, u32[]{:S(2)}) collective-permute-start(bf16[1,64,2048]{1,2,0:T(8,128)(2,1)S(1)} %get-tuple-element.146), channel_id=1, source_target_pairs={{0,1},{1,2},{2,3},{3,4},{4,5},{5,6},{6,7},{7,8},{8,9},{9,10},{10,1... | collective-permute-start | bytes 786440 | tf_op jit(solution)/shard_map/ppermute | solution.py:29
  255.4 1.5 collective-permute-start.3
  258.2 5.5 %collective-permute-done.2 = bf16[1,64,2048]{1,2,0:T(8,128)(2,1)S(1)} collective-permute-done((bf16[1,64,2048]{1,2,0:T(8,128)(2,1)S(1)}, bf16[1,64,2048]{1,2,0:T(8,128)(2,1)S(1)}, u32[]{:S(2)}, u32[]{:S(2)}) %collective-permute-start.2) | collective-permute-done | bytes 262176 | tf_op jit(solution)/shard_map/ppermute | solution.py:29
  265.1 5.4 %scatter-add.6 = f32[1,128,2048]{1,2,0:T(8,128)} dynamic-update-slice(f32[1,128,2048]{1,2,0:T(8,128)} %fusion.29, f32[1,64,2048]{1,2,0:T(8,128)} %fusion.31, s32[]{:T(128)} %constant.131.clone.1, s32[]{:T(128)} %constant.131.clone.1, s32[]{:T(128)} %constant.131.clone.1) | dynamic-update-slice | bytes 1048580 | tf_op jit(solution)/shard_map/scatter-add | solution.py:212
  270.6 2.8 slice_add_fusion
  273.4 8.6 %scatter-add.9 = f32[1,128,2048]{1,2,0:T(8,128)S(1)} dynamic-update-slice(f32[1,128,2048]{1,2,0:T(8,128)S(1)} %copy-done.5, f32[1,64,2048]{1,2,0:T(8,128)} %slice_add_fusion, s32[]{:T(128)} %constant.131.clone.1, s32[]{:T(128)} %constant.142.clone.1, s32[]{:T(128)} %constant.131.clone.1) | dynamic-update-slice | bytes 1048580 | tf_op jit(solution)/shard_map/scatter-add | solution.py:213
  282.1 22.0 %all_to_all.57 = f32[128,16,2,64]{0,3,2,1:T(8,128)} all-to-all(f32[128,16,2,64]{0,3,2,1:T(8,128)S(1)} %copy.194), channel_id=1, replica_groups=mesh['dp'=16,'seq'=16] {'seq'}, dimensions={1} | all-to-all | bytes 2097152 | tf_op jit(solution)/shard_map/all_to_all | solution.py:215
  305.3 3.5 all-to-all-start.5
  308.8 1.8 copy.195
  310.7 3.7 fusion.16
  314.4 2.3 fusion.25
  316.7 8.2 %all-to-all-start.3 = ((f32[16,16,4,128]{3,2,1,0:T(4,128)}), f32[16,16,4,128]{3,2,1,0:T(4,128)S(1)}, u32[]{:S(2)}, u32[]{:S(2)}) async-start(f32[16,16,4,128]{3,2,1,0:T(4,128)} %bitcast.269), calls=%async_computation.3 | async-start | bytes 1048576 | tf_op jit(solution)/shard_map/all_to_all | solution.py:221
  324.9 17.3 %all-to-all-done.3 = f32[16,16,4,128]{3,2,1,0:T(4,128)S(1)} async-done(((f32[16,16,4,128]{3,2,1,0:T(4,128)}), f32[16,16,4,128]{3,2,1,0:T(4,128)S(1)}, u32[]{:S(2)}, u32[]{:S(2)}) %all-to-all-start.3) | async-done | bytes 524320 | tf_op jit(solution)/shard_map/all_to_all | solution.py:221
  342.8 3.3 all-to-all-start.6
  346.8 5.9 %all-to-all-done.6 = f32[16,1,128]{2,1,0:T(1,128)S(1)} async-done(((f32[16,1,128]{2,1,0:T(1,128)}), f32[16,1,128]{2,1,0:T(1,128)S(1)}, u32[]{:S(2)}, u32[]{:S(2)}) %all-to-all-start.6) | async-done | bytes 8224 | tf_op jit(solution)/shard_map/all_to_all | solution.py:93
  352.7 6.9 %all-to-all-start.4 = ((f32[16,4,128]{2,1,0:T(4,128)}), f32[16,4,128]{2,1,0:T(4,128)S(1)}, u32[]{:S(2)}, u32[]{:S(2)}) async-start(f32[16,4,128]{2,1,0:T(4,128)} %reduce_sum.85), calls=%async_computation.4 | async-start | bytes 65536 | tf_op jit(solution)/shard_map/all_to_all | solution.py:222
  359.7 6.4 %all-to-all-done.4 = f32[16,4,128]{2,1,0:T(4,128)S(1)} async-done(((f32[16,4,128]{2,1,0:T(4,128)}), f32[16,4,128]{2,1,0:T(4,128)S(1)}, u32[]{:S(2)}, u32[]{:S(2)}) %all-to-all-start.4) | async-done | bytes 32800 | tf_op jit(solution)/shard_map/all_to_all | solution.py:222
  (112 shorter events, 46.5 us)
Async XLA Ops:
  7.2 206.3 %copy-start = (bf16[1024,1024]{1,0:T(8,128)(2,1)S(1)}, bf16[1024,1024]{1,0:T(8,128)(2,1)}, u32[]{:S(2)}) copy-start(bf16[1024,1024]{1,0:T(8,128)(2,1)} %param.23) | copy-start | bytes 6291460
  7.2 143.5 %all-gather.8.cloned.1.call-start = ((), (), s32[]{:S(2)}) async-start(), calls=%async_computation.8 | async-start | bytes 8912896 | tf_op jit(solution)/shard_map/all_gather | solution.py:117
  34.4 3.9 %copy-start.3 = (bf16[1,128,1024]{2,1,0:T(8,128)(2,1)}, bf16[1,128,1024]{2,1,0:T(8,128)(2,1)S(1)}, u32[]{:S(2)}) copy-start(bf16[1,128,1024]{2,1,0:T(8,128)(2,1)S(1)} %multiply_convert_fusion.1) | copy-start | bytes 786436
  39.5 28.9 %copy-start.10 = (s32[1,2048]{1,0:T(1,128)S(1)}, s32[1,2048]{1,0:T(1,128)}, u32[]{:S(2)}) copy-start(s32[1,2048]{1,0:T(1,128)} %param.19) | copy-start | bytes 24580
  62.2 15.2 %all-to-all-start = ((bf16[16,1,128,3,1,64]{2,5,3,4,1,0:T(8,128)(2,1)}), bf16[16,1,128,3,1,64]{2,5,3,4,1,0:T(8,128)(2,1)S(1)}, u32[]{:S(2)}, u32[]{:S(2)}) async-start(bf16[16,1,128,3,1,64]{2,5,3,4,1,0:T(8,128)(2,1)} %fusion.58), calls=%async_computation | async-start | bytes 1572864 | tf_op jit(solution)/shard_map/all_to_all | solution.py:136
  67.0 243.7 %all-gather.6.cloned.1.call-start = ((), (), s32[]{:S(2)}) async-start(), calls=%async_computation.7 | async-start | bytes 4456448 | tf_op jit(solution)/shard_map/all_gather | solution.py:217
  85.1 1.0 copy-start.8
  89.5 1.0 copy-start.8
  93.9 1.0 copy-start.8
  98.2 1.0 copy-start.8
  103.2 21.9 %copy-start.11 = (u32[256]{0:T(256)S(1)}, u32[256]{0:T(256)}, u32[]{:S(2)}) copy-start(u32[256]{0:T(256)} %constant.155) | copy-start | bytes 3076
  121.5 27.8 %all-to-all-start.1 = ((bf16[16,2,4096]{2,1,0:T(2,128)(2,1)}), bf16[16,2,4096]{2,1,0:T(2,128)(2,1)S(1)}, u32[]{:S(2)}, u32[]{:S(2)}) async-start(bf16[16,2,4096]{2,1,0:T(2,128)(2,1)} %reshape.460), calls=%async_computation.1 | async-start | bytes 524288 | tf_op jit(solution)/shard_map/all_to_all | solution.py:142
  182.1 4.0 %copy-start.4 = (bf16[1,128,1024]{2,1,0:T(8,128)(2,1)S(1)}, bf16[1,128,1024]{2,1,0:T(8,128)(2,1)}, u32[]{:S(2)}) copy-start(bf16[1,128,1024]{2,1,0:T(8,128)(2,1)} %copy-done.3) | copy-start | bytes 786436
  186.1 2.2 copy-start.6
  188.3 7.0 %copy-start.7 = (bf16[1,256,4,1024]{3,1,2,0:T(8,128)(2,1)S(1)}, bf16[1,256,4,1024]{3,1,2,0:T(8,128)(2,1)}, u32[]{:S(2)}) copy-start(bf16[1,256,4,1024]{3,1,2,0:T(8,128)(2,1)} %get-tuple-element.144) | copy-start | bytes 6291460
  189.7 15.4 %collective-permute-start = (bf16[1,64,2048]{2,1,0:T(8,128)(2,1)}, bf16[1,64,2048]{2,1,0:T(8,128)(2,1)}, u32[]{:S(2)}, u32[]{:S(2)}) collective-permute-start(bf16[1,64,2048]{2,1,0:T(8,128)(2,1)} %get-tuple-element.152), channel_id=1, source_target_pairs={{0,1},{1,2},{2,3},{3,4},{4,5},{5,6},{6,7},{7,8},{8,9},{9,10},{10,1... | collective-permute-start | bytes 786440 | tf_op jit(solution)/shard_map/ppermute | solution.py:18
  193.8 11.3 %collective-permute-start.1 = (bf16[1,64,2048]{2,1,0:T(8,128)(2,1)}, bf16[1,64,2048]{2,1,0:T(8,128)(2,1)}, u32[]{:S(2)}, u32[]{:S(2)}) collective-permute-start(bf16[1,64,2048]{2,1,0:T(8,128)(2,1)} %get-tuple-element.153), channel_id=1, source_target_pairs={{1,0},{2,1},{3,2},{4,3},{5,4},{6,5},{7,6},{8,7},{9,8},{10,9},{11,1... | collective-permute-start | bytes 786440 | tf_op jit(solution)/shard_map/ppermute | solution.py:21
  210.7 2.3 copy-start.2
  215.5 2.0 copy-start.9
  251.4 12.4 %collective-permute-start.2 = (bf16[1,64,2048]{1,2,0:T(8,128)(2,1)S(1)}, bf16[1,64,2048]{1,2,0:T(8,128)(2,1)S(1)}, u32[]{:S(2)}, u32[]{:S(2)}) collective-permute-start(bf16[1,64,2048]{1,2,0:T(8,128)(2,1)S(1)} %get-tuple-element.146), channel_id=1, source_target_pairs={{0,1},{1,2},{2,3},{3,4},{4,5},{5,6},{6,7},{7,8},{8,9},{9,10},{10,1... | collective-permute-start | bytes 786440 | tf_op jit(solution)/shard_map/ppermute | solution.py:29
  255.4 15.2 %collective-permute-start.3 = (bf16[1,64,2048]{1,2,0:T(8,128)(2,1)}, bf16[1,64,2048]{1,2,0:T(8,128)(2,1)}, u32[]{:S(2)}, u32[]{:S(2)}) collective-permute-start(bf16[1,64,2048]{1,2,0:T(8,128)(2,1)} %get-tuple-element.145), channel_id=1, source_target_pairs={{1,0},{2,1},{3,2},{4,3},{5,4},{6,5},{7,6},{8,7},{9,8},{10,9},{11,1... | collective-permute-start | bytes 786440 | tf_op jit(solution)/shard_map/ppermute | solution.py:29
  270.6 2.8 copy-start.5
  305.3 11.4 %all-to-all-start.5 = ((f32[16,1,128]{2,1,0:T(1,128)}), f32[16,1,128]{2,1,0:T(1,128)S(1)}, u32[]{:S(2)}, u32[]{:S(2)}) async-start(f32[16,1,128]{2,1,0:T(1,128)} %broadcast_in_dim.59), calls=%async_computation.5 | async-start | bytes 16384 | tf_op jit(solution)/shard_map/all_to_all | solution.py:91
  310.7 3.7 copy-start.1
  316.7 25.5 %all-to-all-start.3 = ((f32[16,16,4,128]{3,2,1,0:T(4,128)}), f32[16,16,4,128]{3,2,1,0:T(4,128)S(1)}, u32[]{:S(2)}, u32[]{:S(2)}) async-start(f32[16,16,4,128]{3,2,1,0:T(4,128)} %bitcast.269), calls=%async_computation.3 | async-start | bytes 1048576 | tf_op jit(solution)/shard_map/all_to_all | solution.py:221
  342.8 10.0 %all-to-all-start.6 = ((f32[16,1,128]{2,1,0:T(1,128)}), f32[16,1,128]{2,1,0:T(1,128)S(1)}, u32[]{:S(2)}, u32[]{:S(2)}) async-start(f32[16,1,128]{2,1,0:T(1,128)} %broadcast_in_dim.88), calls=%async_computation.6 | async-start | bytes 16384 | tf_op jit(solution)/shard_map/all_to_all | solution.py:93
  352.7 13.3 %all-to-all-start.4 = ((f32[16,4,128]{2,1,0:T(4,128)}), f32[16,4,128]{2,1,0:T(4,128)S(1)}, u32[]{:S(2)}, u32[]{:S(2)}) async-start(f32[16,4,128]{2,1,0:T(4,128)} %reduce_sum.85), calls=%async_computation.4 | async-start | bytes 65536 | tf_op jit(solution)/shard_map/all_to_all | solution.py:222
Sparse Core Ops, SparseCore 0:
  30.7 62.3 all-gather.7
  95.6 55.8 all-gather.5
